TPU v7x, 32 devices: a whole 2x2x4 slice. The times are simulated.
32 devices in a mesh: row: 8 (over z, x), col: 4 (over y, core).
Axes of the slice: x: 2, y: 2, z: 4, core: 2. Of those that a mesh axis runs over, the one named last changes fastest.
Arguments:
- low_rhs: bfloat16 [32, 512, 128], P(('row', 'col')), may hold values from -6 to 6
- low_inv: bfloat16 [32, 512, 512], P(('row', 'col'))
- low_tiles: bfloat16 [32, 4, 512, 512], P(('row', 'col')), may hold values from -0.03125 to 0.03125
- tile_rows: int32 [32, 4], P(('row', 'col')), may hold values from -1 to 3, as said below
- tile_cols: int32 [32, 4], P(('row', 'col')), may hold values from 0 to 31, as said below
- top_rhs: bfloat16 [4, 512, 128], P(None, 'row'), may hold values from -6 to 6
- top_inv: bfloat16 [4, 512, 512], P(None, 'row')
- top_tiles: bfloat16 [6, 512, 512], P(None, 'row'), may hold values from -0.125 to 0.125
Outputs:
- low_solution: float32 [32, 512, 128], P(('row', 'col'))
- top_solution: float32 [4, 512, 128], P(None, 'row')
Inputs may be any that keep to these rules, and one draw needn't show every extreme that they name: `tile_rows`: in each block's list of 4 slots the used slots come first and name top-level blocks; the remaining slots hold -1. Some list has only its first slot used and some list is full. Slot s of block j names a block of j's aligned group of 4 blocks (j // 4 == tile_cols[j, s] // 4); an empty slot names j itself.
All inputs are finite; a program needn't handle non-finite values.
Results may differ from a plain program's by a relative error of at most 0.022.
Values may be sent and summed in bfloat16 or wider, within the bound.
No kernel may reach another device: no remote copies, remote signals or barrier semaphores. Data moves between devices by JAX's collectives and lax.ppermute only.
A program may use at most 64 MiB of HBM per device.

v0:
```python
import jax
import jax.numpy as jnp
from jax import lax
from jax.sharding import PartitionSpec as P


def local(low_rhs, low_inv, low_tiles, tile_rows, tile_cols, top_rhs, top_inv, top_tiles):
    peers = lax.axis_size("col")
    levels = top_rhs.shape[0]
    share = top_rhs.shape[1]
    position = lax.axis_index("row")
    slot_rows = tile_rows[0]
    slot_cols = tile_cols[0] % peers
    alive = slot_rows >= 0
    safe_rows = jnp.maximum(slot_rows, 0)
    own_tiles = low_tiles[0]
    low_forward = jnp.dot(low_inv[0], low_rhs[0], preferred_element_type=jnp.float32).astype(
        jnp.bfloat16
    )
    panels = lax.all_gather(low_forward[None], "col", axis=0, tiled=True)
    products = jnp.einsum(
        "sab,sbk->sak", own_tiles, panels[slot_cols], preferred_element_type=jnp.float32
    )
    pick_level = (slot_rows[:, None] == jnp.arange(levels, dtype=jnp.int32)[None, :]).astype(
        jnp.float32
    )
    coupling = jnp.einsum("st,sak->tak", pick_level, products, precision=lax.Precision.HIGHEST)
    whole_sum = lax.psum(coupling.astype(jnp.bfloat16), "col")
    coupled = lax.psum_scatter(whole_sum, "row", scatter_dimension=1, tiled=True).astype(
        jnp.float32
    )
    top_back = [None] * levels
    top_slices = [None] * levels
    top_forward = []
    for level in range(levels):
        residue = top_rhs[level].astype(jnp.float32) - coupled[level]
        if level > 0:
            first = level * (level - 1) // 2
            earlier = jnp.stack(top_forward)
            residue = residue - jnp.einsum(
                "uab,ubk->ak",
                top_tiles[first : first + level],
                earlier,
                preferred_element_type=jnp.float32,
            )
        whole_residue = lax.all_gather(residue.astype(jnp.bfloat16), "row", axis=0, tiled=True)
        solved_part = jnp.dot(
            top_inv[level], whole_residue, preferred_element_type=jnp.float32
        ).astype(jnp.bfloat16)
        top_forward.append(lax.all_gather(solved_part, "row", axis=0, tiled=True))
    for level in reversed(range(levels)):
        update = lax.dynamic_slice_in_dim(top_forward[level], position * share, share, 0).astype(
            jnp.float32
        )
        if level < levels - 1:
            later = list(range(level + 1, levels))
            tiles_below = jnp.stack([top_tiles[k * (k - 1) // 2 + level] for k in later])
            slices_below = jnp.stack(
                [lax.dynamic_slice_in_dim(top_back[k], position * share, share, 0) for k in later]
            )
            partial_term = jnp.einsum(
                "kab,kac->bc", tiles_below, slices_below, preferred_element_type=jnp.float32
            )
            update = update - lax.psum_scatter(
                partial_term.astype(jnp.bfloat16), "row", scatter_dimension=0, tiled=True
            ).astype(jnp.float32)
        local_part = jnp.einsum(
            "ab,ac->bc",
            top_inv[level],
            update.astype(jnp.bfloat16),
            preferred_element_type=jnp.float32,
        )
        solution = lax.psum(local_part.astype(jnp.bfloat16), "row").astype(jnp.float32)
        top_slices[level] = lax.dynamic_slice_in_dim(solution, position * share, share, 0)
        top_back[level] = solution.astype(jnp.bfloat16)
    back_stack = jnp.stack(top_back)
    products_back = jnp.einsum(
        "sab,sak->sbk", own_tiles, back_stack[safe_rows], preferred_element_type=jnp.float32
    )
    pick_peer = (
        (slot_cols[:, None] == jnp.arange(peers, dtype=jnp.int32)[None, :]) & alive[:, None]
    ).astype(jnp.float32)
    terms = jnp.einsum("sp,sbk->pbk", pick_peer, products_back, precision=lax.Precision.HIGHEST)
    returned = lax.psum_scatter(
        terms.astype(jnp.bfloat16), "col", scatter_dimension=0, tiled=True
    ).astype(jnp.float32)
    low_update = (low_forward.astype(jnp.float32) - returned[0]).astype(jnp.bfloat16)
    low_solution = jnp.einsum(
        "ab,ac->bc", low_inv[0], low_update, preferred_element_type=jnp.float32
    )
    return (low_solution[None], jnp.stack(top_slices))


def solution(mesh):
    in_specs = (
        P(("row", "col"), None, None),
        P(("row", "col"), None, None),
        P(("row", "col"), None, None, None),
        P(("row", "col"), None),
        P(("row", "col"), None),
        P(None, "row", None),
        P(None, "row", None),
        P(None, "row", None),
    )
    out_specs = (P(("row", "col"), None, None), P(None, "row", None))
    return jax.shard_map(local, mesh=mesh, in_specs=in_specs, out_specs=out_specs, check_vma=False)
```

profile of v0, /device:TPU:0, one launch (start us, length us, event | category | flops | bytes accessed | tf_op | source)
XLA Modules:
  0.0 905.1 jit_solution(3152110872918101658)
XLA Ops:
  7.2 1.5 convolution_convert_fusion.1
  8.7 8.7 all-gather
  17.4 0.7 fusion.99
  18.1 1.4 gather_fusion
  19.5 1.9 fusion.4
  21.4 1.3 copy.37
  22.7 3.2 convolution_convert_fusion
  26.0 0.6 dynamic-slice
  27.2 72.4 %all-reduce.18.cloned.1.call-done = bf16[4,512,128]{2,0,1:T(4,128)(2,1)} async-done(((bf16[4,512,128]{2,0,1:T(4,128)(2,1)}), bf16[4,512,128]{2,0,1:T(4,128)(2,1)}) %all-reduce.18.cloned.1.call-update) | async-done | bytes 524304
  99.6 0.9 constant_dynamic-slice_fusion.3
  100.5 0.6 copy.38
  101.2 32.1 %all-reduce.16.cloned.1.call-done = bf16[4,64,128]{2,1,0:T(8,128)(2,1)} async-done(((bf16[4,64,128]{2,1,0:T(8,128)(2,1)}), bf16[4,64,128]{2,1,0:T(8,128)(2,1)}) %all-reduce.16.cloned.1.call-update) | async-done | bytes 65552 | tf_op jit(solution)/shard_map/psum | solution.py:28
  133.2 0.8 convert_element_type.161
  134.1 30.7 %all-gather.1 = bf16[1,512,128]{2,1,0:T(8,128)(2,1)S(1)} all-gather(bf16[1,64,128]{2,1,0:T(8,128)(2,1)S(1)} %fusion.76), channel_id=3, replica_groups=mesh['row'=8,'col'=4] {'row'}, dimensions={1}, use_global_device_ids=true | all-gather | bytes 147456 | tf_op jit(solution)/shard_map/all_gather | solution.py:46
  164.8 0.2 fusion.23
  164.9 30.6 %all_gather.29 = bf16[512,128]{1,0:T(8,128)(2,1)S(1)} all-gather(bf16[64,128]{1,0:T(8,128)(2,1)S(1)} %fusion.23), channel_id=1, replica_groups=mesh['row'=8,'col'=4] {'row'}, dimensions={0}, use_global_device_ids=true | all-gather | bytes 147456 | tf_op jit(solution)/shard_map/all_gather | solution.py:50
  195.5 0.2 fusion.20
  195.6 30.5 %all_gather.30 = bf16[512,128]{1,0:T(8,128)(2,1)S(1)} all-gather(bf16[64,128]{1,0:T(8,128)(2,1)S(1)} %fusion.20), channel_id=1, replica_groups=mesh['row'=8,'col'=4] {'row'}, dimensions={0}, use_global_device_ids=true | all-gather | bytes 147456 | tf_op jit(solution)/shard_map/all_gather | solution.py:46
  226.2 0.2 fusion.24
  226.3 30.6 %all_gather.31 = bf16[512,128]{1,0:T(8,128)(2,1)S(1)} all-gather(bf16[64,128]{1,0:T(8,128)(2,1)S(1)} %fusion.24), channel_id=1, replica_groups=mesh['row'=8,'col'=4] {'row'}, dimensions={0}, use_global_device_ids=true | all-gather | bytes 147456 | tf_op jit(solution)/shard_map/all_gather | solution.py:50
  256.9 0.2 fusion.22
  257.1 30.6 %all_gather.32 = bf16[512,128]{1,0:T(8,128)(2,1)S(1)} all-gather(bf16[64,128]{1,0:T(8,128)(2,1)S(1)} %fusion.22), channel_id=1, replica_groups=mesh['row'=8,'col'=4] {'row'}, dimensions={0}, use_global_device_ids=true | all-gather | bytes 147456 | tf_op jit(solution)/shard_map/all_gather | solution.py:46
  287.7 0.2 fusion.25
  287.8 30.6 %all_gather.33 = bf16[512,128]{1,0:T(8,128)(2,1)S(1)} all-gather(bf16[64,128]{1,0:T(8,128)(2,1)S(1)} %fusion.25), channel_id=1, replica_groups=mesh['row'=8,'col'=4] {'row'}, dimensions={0}, use_global_device_ids=true | all-gather | bytes 147456 | tf_op jit(solution)/shard_map/all_gather | solution.py:50
  318.4 1.0 fusion.21
  319.4 30.5 %all_gather.34 = bf16[512,128]{1,0:T(8,128)(2,1)S(1)} all-gather(bf16[64,128]{1,0:T(8,128)(2,1)S(1)} %fusion.21), channel_id=1, replica_groups=mesh['row'=8,'col'=4] {'row'}, dimensions={0}, use_global_device_ids=true | all-gather | bytes 147456 | tf_op jit(solution)/shard_map/all_gather | solution.py:46
  349.9 0.2 fusion.26
  350.1 30.5 %all_gather.35 = bf16[512,128]{1,0:T(8,128)(2,1)S(1)} all-gather(bf16[64,128]{1,0:T(8,128)(2,1)S(1)} %fusion.26), channel_id=1, replica_groups=mesh['row'=8,'col'=4] {'row'}, dimensions={0}, use_global_device_ids=true | all-gather | bytes 147456 | tf_op jit(solution)/shard_map/all_gather | solution.py:50
  380.6 0.9 fusion.12
  381.5 70.7 %all-reduce.8.cloned.1.call-done = bf16[512,128]{0,1:T(8,128)(2,1)} async-done(((bf16[512,128]{0,1:T(8,128)(2,1)}), bf16[512,128]{0,1:T(8,128)(2,1)}) %all-reduce.8.cloned.1.call-update) | async-done | bytes 131088 | tf_op jit(solution)/shard_map/psum | solution.py:73
  452.2 0.9 constant_dynamic-slice_fusion.2
  453.1 0.9 fusion.13
  454.1 62.9 %reduce-scatter.5.cloned.1.call-done = bf16[64,128]{1,0:T(8,128)(2,1)} async-done(((bf16[512,128]{1,0:T(8,128)(2,1)}), bf16[64,128]{1,0:T(8,128)(2,1)}) %reduce-scatter.5.cloned.1.call-update) | async-done | bytes 16400 | tf_op jit(solution)/shard_map/reduce_scatter | solution.py:64
  516.9 1.6 fusion.14
  518.6 0.7 fusion.104
  519.3 0.1 copy.41
  519.3 70.9 %all-reduce.10.cloned.1.call-done = bf16[512,128]{0,1:T(8,128)(2,1)} async-done(((bf16[512,128]{0,1:T(8,128)(2,1)}), bf16[512,128]{0,1:T(8,128)(2,1)}) %all-reduce.10.cloned.1.call-update) | async-done | bytes 131088 | tf_op jit(solution)/shard_map/psum | solution.py:73
  590.3 0.9 constant_dynamic-slice_fusion.1
  591.2 0.1 copy.40
  591.3 1.8 fusion.10
  593.1 61.9 %reduce-scatter.7.cloned.1.call-done = bf16[64,128]{1,0:T(8,128)(2,1)} async-done(((bf16[512,128]{1,0:T(8,128)(2,1)}), bf16[64,128]{1,0:T(8,128)(2,1)}) %reduce-scatter.7.cloned.1.call-update) | async-done | bytes 16400 | tf_op jit(solution)/shard_map/reduce_scatter | solution.py:64
  655.0 1.6 fusion.15
  656.7 71.8 %all-reduce.12.cloned.1.call-done = bf16[512,128]{0,1:T(8,128)(2,1)} async-done(((bf16[512,128]{0,1:T(8,128)(2,1)}), bf16[512,128]{0,1:T(8,128)(2,1)}) %all-reduce.12.cloned.1.call-update) | async-done | bytes 131088 | tf_op jit(solution)/shard_map/psum | solution.py:73
  728.5 0.8 constant_dynamic-slice_fusion
  729.3 0.1 copy.42
  729.4 1.8 fusion.11
  731.3 62.1 %reduce-scatter.9.cloned.1.call-done = bf16[64,128]{1,0:T(8,128)(2,1)} async-done(((bf16[512,128]{1,0:T(8,128)(2,1)}), bf16[64,128]{1,0:T(8,128)(2,1)}) %reduce-scatter.9.cloned.1.call-update) | async-done | bytes 16400 | tf_op jit(solution)/shard_map/reduce_scatter | solution.py:64
  793.4 1.6 fusion.16
  795.1 71.8 %all-reduce.14.cloned.1.call-done = bf16[512,128]{0,1:T(8,128)(2,1)} async-done(((bf16[512,128]{0,1:T(8,128)(2,1)}), bf16[512,128]{0,1:T(8,128)(2,1)}) %all-reduce.14.cloned.1.call-update) | async-done | bytes 131088 | tf_op jit(solution)/shard_map/psum | solution.py:73
  866.9 1.0 pad_maximum_fusion
  868.0 1.4 gather_fusion.1
  869.3 1.5 fusion.7
  870.8 1.3 copy.43
  872.1 2.4 fusion.90
  874.5 0.9 copy.53
  875.4 0.1 copy.48
  875.5 0.1 copy.47
  875.6 0.1 copy.46
  875.7 0.9 dynamic-slice_convert_fusion
  876.5 0.1 copy.45
  876.6 0.7 pad_maximum_fusion.1
  877.3 19.0 %reduce-scatter.11.cloned.1.call-done = bf16[1,512,128]{2,1,0:T(8,128)(2,1)} async-done(((bf16[4,512,128]{2,1,0:T(8,128)(2,1)}), bf16[1,512,128]{2,1,0:T(8,128)(2,1)}) %reduce-scatter.11.cloned.1.call-update) | async-done | bytes 131088 | tf_op jit(solution)/shard_map/reduce_scatter | solution.py:84
  896.3 1.2 convolution_bitcast_fusion
  897.5 0.8 copy.49
  (62 shorter events, 0.7 us)
Async XLA Ops:
  7.2 12.3 %copy-start = (bf16[1,4,512,512]{3,2,1,0:T(8,128)(2,1)S(1)}, bf16[1,4,512,512]{3,2,1,0:T(8,128)(2,1)}, u32[]{:S(2)}) copy-start(bf16[1,4,512,512]{3,2,1,0:T(8,128)(2,1)} %param.10) | copy-start | bytes 6291460
  7.2 92.4 %all-reduce.18.cloned.1.call-start = ((), (), s32[]{:S(2)}) async-start(), calls=%async_computation.13 | async-start | bytes 1048576
  19.5 3.2 copy-start.14
  21.4 4.6 copy-start.16
  21.4 143.4 %copy-start.2 = (bf16[4,64,512]{2,1,0:T(8,128)(2,1)S(1)}, bf16[4,64,512]{2,1,0:T(8,128)(2,1)}, u32[]{:S(2)}) copy-start(bf16[4,64,512]{2,1,0:T(8,128)(2,1)} %param.14) | copy-start | bytes 786436
  22.7 111.4 %copy-start.13 = (bf16[4,64,128]{2,1,0:T(8,128)(2,1)S(1)}, bf16[4,64,128]{2,1,0:T(8,128)(2,1)}, u32[]{:S(2)}) copy-start(bf16[4,64,128]{2,1,0:T(8,128)(2,1)} %param.13) | copy-start | bytes 196612
  22.7 172.7 %copy-start.3 = (bf16[6,64,512]{2,1,0:T(8,128)(2,1)S(1)}, bf16[6,64,512]{2,1,0:T(8,128)(2,1)}, u32[]{:S(2)}) copy-start(bf16[6,64,512]{2,1,0:T(8,128)(2,1)} %param.15) | copy-start | bytes 1179652
  25.9 107.3 %all-reduce.16.cloned.1.call-start = ((), (), s32[]{:S(2)}) async-start(), calls=%async_computation.12 | async-start | bytes 131072 | tf_op jit(solution)/shard_map/psum | solution.py:28
  101.1 351.1 %all-reduce.8.cloned.1.call-start = ((), (), s32[]{:S(2)}) async-start(), calls=%async_computation.4 | async-start | bytes 262144 | tf_op jit(solution)/shard_map/psum | solution.py:73
  256.9 124.6 %copy-start.12 = (bf16[512,128]{1,0:T(8,128)(2,1)}, bf16[512,128]{1,0:T(8,128)(2,1)S(1)}, u32[]{:S(2)}) copy-start(bf16[512,128]{1,0:T(8,128)(2,1)S(1)} %all_gather.31) | copy-start | bytes 393220
  318.4 411.0 %slice-start = ((bf16[6,64,512]{2,1,0:T(8,128)(2,1)}), bf16[2,64,512]{2,1,0:T(8,128)(2,1)S(1)}, s32[]{:S(2)}) async-start(bf16[6,64,512]{2,1,0:T(8,128)(2,1)} %param.15), calls=%async_computation.14 | async-start | bytes 262144 | tf_op jit(solution)/shard_map/slice | solution.py:57
  319.4 411.9 %copy-start.15 = (s32[1,4]{1,0:T(1,128)S(1)}, s32[1,4]{1,0:T(1,128)}, u32[]{:S(2)}) copy-start(s32[1,4]{1,0:T(1,128)} %param.12) | copy-start | bytes 52
  381.5 135.4 %reduce-scatter.5.cloned.1.call-start = ((), (), s32[]{:S(2)}) async-start(), calls=%async_computation.5 | async-start | bytes 147456 | tf_op jit(solution)/shard_map/reduce_scatter | solution.py:64
  452.2 414.7 %copy-start.10 = (bf16[512,128]{0,1:T(8,128)(2,1)S(1)}, bf16[512,128]{0,1:T(8,128)(2,1)}, u32[]{:S(2)}) copy-start(bf16[512,128]{0,1:T(8,128)(2,1)} %all-reduce.8.cloned.1.call-done) | copy-start | bytes 393220
  453.1 414.8 %copy-start.4 = (bf16[64,128]{0,1:T(8,128)(2,1)}, bf16[64,128]{0,1:T(8,128)(2,1)S(1)}, u32[]{:S(2)}) copy-start(bf16[64,128]{0,1:T(8,128)(2,1)S(1)} %constant_dynamic-slice_fusion.2) | copy-start | bytes 49156
  454.0 136.2 %all-reduce.10.cloned.1.call-start = ((), (), s32[]{:S(2)}) async-start(), calls=%async_computation.6 | async-start | bytes 262144 | tf_op jit(solution)/shard_map/psum | solution.py:73
  518.5 136.5 %reduce-scatter.7.cloned.1.call-start = ((), (), s32[]{:S(2)}) async-start(), calls=%async_computation.7 | async-start | bytes 147456 | tf_op jit(solution)/shard_map/reduce_scatter | solution.py:64
  590.3 276.6 %copy-start.11 = (bf16[512,128]{0,1:T(8,128)(2,1)S(1)}, bf16[512,128]{0,1:T(8,128)(2,1)}, u32[]{:S(2)}) copy-start(bf16[512,128]{0,1:T(8,128)(2,1)} %all-reduce.10.cloned.1.call-done) | copy-start | bytes 393220
  591.2 276.8 %copy-start.6 = (bf16[64,128]{0,1:T(8,128)(2,1)}, bf16[64,128]{0,1:T(8,128)(2,1)S(1)}, u32[]{:S(2)}) copy-start(bf16[64,128]{0,1:T(8,128)(2,1)S(1)} %constant_dynamic-slice_fusion.1) | copy-start | bytes 49156
  593.0 135.4 %all-reduce.12.cloned.1.call-start = ((), (), s32[]{:S(2)}) async-start(), calls=%async_computation.8 | async-start | bytes 262144 | tf_op jit(solution)/shard_map/psum | solution.py:73
  656.6 136.8 %reduce-scatter.9.cloned.1.call-start = ((), (), s32[]{:S(2)}) async-start(), calls=%async_computation.9 | async-start | bytes 147456 | tf_op jit(solution)/shard_map/reduce_scatter | solution.py:64
  729.3 138.6 %copy-start.8 = (bf16[64,128]{0,1:T(8,128)(2,1)}, bf16[64,128]{0,1:T(8,128)(2,1)S(1)}, u32[]{:S(2)}) copy-start(bf16[64,128]{0,1:T(8,128)(2,1)S(1)} %constant_dynamic-slice_fusion) | copy-start | bytes 49156
  731.2 135.7 %all-reduce.14.cloned.1.call-start = ((), (), s32[]{:S(2)}) async-start(), calls=%async_computation.10 | async-start | bytes 262144 | tf_op jit(solution)/shard_map/psum | solution.py:73
  795.0 101.3 %reduce-scatter.11.cloned.1.call-start = ((), (), s32[]{:S(2)}) async-start(), calls=%async_computation.11 | async-start | bytes 655360 | tf_op jit(solution)/shard_map/reduce_scatter | solution.py:84
  872.1 3.3 copy-start.5
  872.1 3.3 copy-start.7
  872.1 3.4 copy-start.9
  872.1 24.2 %copy-start.1 = (bf16[1,512,512]{2,1,0:T(8,128)(2,1)S(1)}, bf16[1,512,512]{2,1,0:T(8,128)(2,1)}, u32[]{:S(2)}) copy-start(bf16[1,512,512]{2,1,0:T(8,128)(2,1)} %param.9) | copy-start | bytes 1572868
Sparse Core Ops, SparseCore 0:
  26.0 73.4 all-reduce.17
  102.5 30.7 all-reduce.15
  381.6 70.5 all-reduce.7
  455.9 60.9 reduce-scatter.4
  520.7 69.5 all-reduce.9
  594.0 60.9 reduce-scatter.6
  658.9 69.5 all-reduce.11
  732.4 60.9 reduce-scatter.8
  797.3 69.5 all-reduce.13
  875.5 20.7 reduce-scatter.10
where the time goes:
time: 906 us; the launch traced here: 905 us
  waiting for transfers between devices  596 us (66%)
  blocking collectives  253 us (28%)
  matrix products  23.5 us (3%)
  between operations  15.1 us (2%)
  local copies, waits for them, and re-layouts  13.2 us (1%)
    psum x4, waiting for transfers between devices, local(): lax.psum(local_part.astype(jnp.bfloat16), 'row').astype(jnp.float32)  285 us
    reduce_scatter x3, waiting for transfers between devices, local(): lax.psum_scatter(partial_term.astype(jnp.bfloat16), 'row', scatter_dimens...  187 us
    all_gather x4, blocking collectives, local(): lax.all_gather(residue.astype(jnp.bfloat16), 'row', axis=0, tiled=True)  122 us
    all_gather x4, blocking collectives, local(): top_forward.append(lax.all_gather(solved_part, 'row', axis=0, tiled=True))  122 us
    unnamed x11, waiting for transfers between devices  72.5 us
    psum x1, waiting for transfers between devices, local(): whole_sum = lax.psum(coupling.astype(jnp.bfloat16), 'col')  32.1 us
    reduce_scatter x1, waiting for transfers between devices, local(): lax.psum_scatter(terms.astype(jnp.bfloat16), 'col', scatter_dimension=0,...  19 us
  transfers between devices with their start and end apart: 10, of which 10 were waited for; matrix products, arithmetic and copies ran while one was open for 0% of the time, Pallas kernels for 0%

commit v1 on v0

--- a/solution.py
+++ b/solution.py
@@ -43,7 +43,12 @@
                 earlier,
                 preferred_element_type=jnp.float32,
             )
-        whole_residue = lax.all_gather(residue.astype(jnp.bfloat16), "row", axis=0, tiled=True)
+        whole_residue = jnp.concatenate(
+            lax.all_to_all(
+                jnp.stack([residue.astype(jnp.bfloat16)] * lax.axis_size("row")), "row", 0, 0
+            ),
+            axis=0,
+        )
         solved_part = jnp.dot(
             top_inv[level], whole_residue, preferred_element_type=jnp.float32
         ).astype(jnp.bfloat16)

time: 906 us -> 826 us (0.912)
  blocking collectives: 253 us -> 163 us
    all_gather x4 -> x0, blocking collectives: 122 us -> none  [local(): lax.all_gather(residue.astype(jnp.bfloat16), 'row', axis=0, tiled=True)]
    all_to_all x0 -> x3, blocking collectives: none -> 32.1 us  [local(): lax.all_to_all(jnp.stack([residue.astype(jnp.bfloat16)] * lax.axis_size('...]
  transfers between devices with their start and end apart: 10 -> 11, of which waited for: 10 -> 11; matrix products, arithmetic and copies ran while one was open for 0% -> 0% of each run, Pallas kernels for 0% -> 0%
where the time goes in v1:
time: 826 us; the launch traced here: 825 us
  waiting for transfers between devices  600 us (73%)
  blocking collectives  163 us (20%)
  matrix products  24.2 us (3%)
  between operations  15.1 us (2%)
  local copies, waits for them, and re-layouts  14.6 us (2%)
    psum x4, waiting for transfers between devices, local(): lax.psum(local_part.astype(jnp.bfloat16), 'row').astype(jnp.float32)  282 us
    reduce_scatter x3, waiting for transfers between devices, local(): lax.psum_scatter(partial_term.astype(jnp.bfloat16), 'row', scatter_dimens...  187 us
    all_gather x4, blocking collectives, local(): top_forward.append(lax.all_gather(solved_part, 'row', axis=0, tiled=True))  123 us
    unnamed x11, waiting for transfers between devices  72.5 us
    all_to_all x3, blocking collectives, local(): lax.all_to_all(jnp.stack([residue.astype(jnp.bfloat16)] * lax.axis_size('...  32.1 us
    psum x1, waiting for transfers between devices, local(): whole_sum = lax.psum(coupling.astype(jnp.bfloat16), 'col')  32.1 us
    reduce_scatter x1, waiting for transfers between devices, local(): lax.psum_scatter(terms.astype(jnp.bfloat16), 'col', scatter_dimension=0,...  19.1 us
  transfers between devices with their start and end apart: 11, of which 11 were waited for; matrix products, arithmetic and copies ran while one was open for 0% of the time, Pallas kernels for 0%

profile of v1, /device:TPU:0, one launch (start us, length us, event | category | flops | bytes accessed | tf_op | source)
XLA Modules:
  0.0 824.9 jit_solution(13348220008663568363)
XLA Ops:
  7.2 1.5 convolution_convert_fusion.1
  8.7 8.7 %all-gather = bf16[2048,128]{1,0:T(8,128)(2,1)S(1)} all-gather(bf16[512,128]{1,0:T(8,128)(2,1)S(1)} %convolution_convert_fusion.1), channel_id=2, replica_groups=mesh['row'=8,'col'=4] {'col'}, dimensions={0}, use_global_device_ids=true | all-gather | bytes 655360 | tf_op jit(solution)/shard_map/all_gather | solution.py:20
  17.4 0.7 fusion.99
  18.1 1.4 gather_fusion
  19.5 1.9 fusion.4
  21.4 1.3 copy.37
  22.7 3.2 convolution_convert_fusion
  26.0 0.6 dynamic-slice
  27.2 72.3 %all-reduce.18.cloned.1.call-done = bf16[4,512,128]{2,0,1:T(4,128)(2,1)} async-done(((bf16[4,512,128]{2,0,1:T(4,128)(2,1)}), bf16[4,512,128]{2,0,1:T(4,128)(2,1)}) %all-reduce.18.cloned.1.call-update) | async-done | bytes 524304
  99.6 0.9 constant_dynamic-slice_fusion.3
  100.4 0.6 copy.38
  101.1 32.1 %all-reduce.16.cloned.1.call-done = bf16[4,64,128]{2,1,0:T(8,128)(2,1)} async-done(((bf16[4,64,128]{2,1,0:T(8,128)(2,1)}), bf16[4,64,128]{2,1,0:T(8,128)(2,1)}) %all-reduce.16.cloned.1.call-update) | async-done | bytes 65552 | tf_op jit(solution)/shard_map/psum | solution.py:28
  133.2 0.8 convert_element_type.159
  134.1 12.7 %all_to_all.20 = bf16[8,64,128]{2,1,0:T(8,128)(2,1)S(1)} all-to-all(bf16[8,64,128]{2,1,0:T(8,128)(2,1)S(1)} %stack.56), channel_id=1, replica_groups=mesh['row'=8,'col'=4] {'row'}, dimensions={0} | all-to-all | bytes 262144 | tf_op jit(solution)/shard_map/all_to_all | solution.py:47
  146.8 0.2 fusion.23
  146.9 30.6 %all_gather.16 = bf16[512,128]{1,0:T(8,128)(2,1)S(1)} all-gather(bf16[64,128]{1,0:T(8,128)(2,1)S(1)} %fusion.23), channel_id=1, replica_groups=mesh['row'=8,'col'=4] {'row'}, dimensions={0}, use_global_device_ids=true | all-gather | bytes 147456 | tf_op jit(solution)/shard_map/all_gather | solution.py:55
  177.6 0.2 fusion.20
  177.7 9.7 %all_to_all.21 = bf16[8,64,128]{2,1,0:T(8,128)(2,1)S(1)} all-to-all(bf16[8,64,128]{2,1,0:T(8,128)(2,1)S(1)} %stack.58), channel_id=1, replica_groups=mesh['row'=8,'col'=4] {'row'}, dimensions={0} | all-to-all | bytes 262144 | tf_op jit(solution)/shard_map/all_to_all | solution.py:47
  187.5 0.2 fusion.24
  187.6 30.6 %all_gather.17 = bf16[512,128]{1,0:T(8,128)(2,1)S(1)} all-gather(bf16[64,128]{1,0:T(8,128)(2,1)S(1)} %fusion.24), channel_id=1, replica_groups=mesh['row'=8,'col'=4] {'row'}, dimensions={0}, use_global_device_ids=true | all-gather | bytes 147456 | tf_op jit(solution)/shard_map/all_gather | solution.py:55
  218.3 0.9 fusion.22
  219.2 9.7 %all_to_all.22 = bf16[8,64,128]{2,1,0:T(8,128)(2,1)S(1)} all-to-all(bf16[8,64,128]{2,1,0:T(8,128)(2,1)S(1)} %stack.63), channel_id=1, replica_groups=mesh['row'=8,'col'=4] {'row'}, dimensions={0} | all-to-all | bytes 262144 | tf_op jit(solution)/shard_map/all_to_all | solution.py:47
  228.9 0.2 fusion.25
  229.1 30.7 %all_gather.18 = bf16[512,128]{1,0:T(8,128)(2,1)S(1)} all-gather(bf16[64,128]{1,0:T(8,128)(2,1)S(1)} %fusion.25), channel_id=1, replica_groups=mesh['row'=8,'col'=4] {'row'}, dimensions={0}, use_global_device_ids=true | all-gather | bytes 147456 | tf_op jit(solution)/shard_map/all_gather | solution.py:55
  259.8 0.7 copy-done.13
  260.4 0.9 fusion.21
  261.4 0.7 stack.130
  262.0 3.5 all-to-all-start.3
  265.6 7.3 all-to-all-done.3
  272.9 0.2 fusion.26
  273.1 30.6 %all_gather.19 = bf16[512,128]{1,0:T(8,128)(2,1)S(1)} all-gather(bf16[64,128]{1,0:T(8,128)(2,1)S(1)} %fusion.26), channel_id=1, replica_groups=mesh['row'=8,'col'=4] {'row'}, dimensions={0}, use_global_device_ids=true | all-gather | bytes 147456 | tf_op jit(solution)/shard_map/all_gather | solution.py:55
  303.7 0.9 fusion.12
  304.6 67.2 %all-reduce.8.cloned.1.call-done = bf16[512,128]{0,1:T(8,128)(2,1)} async-done(((bf16[512,128]{0,1:T(8,128)(2,1)}), bf16[512,128]{0,1:T(8,128)(2,1)}) %all-reduce.8.cloned.1.call-update) | async-done | bytes 131088 | tf_op jit(solution)/shard_map/psum | solution.py:78
  371.8 0.9 constant_dynamic-slice_fusion.2
  372.7 0.9 fusion.13
  373.7 62.8 %reduce-scatter.5.cloned.1.call-done = bf16[64,128]{1,0:T(8,128)(2,1)} async-done(((bf16[512,128]{1,0:T(8,128)(2,1)}), bf16[64,128]{1,0:T(8,128)(2,1)}) %reduce-scatter.5.cloned.1.call-update) | async-done | bytes 16400 | tf_op jit(solution)/shard_map/reduce_scatter | solution.py:69
  436.6 1.6 fusion.14
  438.2 0.7 fusion.104
  438.9 0.1 copy.41
  439.0 70.9 %all-reduce.10.cloned.1.call-done = bf16[512,128]{0,1:T(8,128)(2,1)} async-done(((bf16[512,128]{0,1:T(8,128)(2,1)}), bf16[512,128]{0,1:T(8,128)(2,1)}) %all-reduce.10.cloned.1.call-update) | async-done | bytes 131088 | tf_op jit(solution)/shard_map/psum | solution.py:78
  509.9 0.9 constant_dynamic-slice_fusion.1
  510.8 0.1 copy.40
  510.9 1.8 fusion.10
  512.7 61.9 %reduce-scatter.7.cloned.1.call-done = bf16[64,128]{1,0:T(8,128)(2,1)} async-done(((bf16[512,128]{1,0:T(8,128)(2,1)}), bf16[64,128]{1,0:T(8,128)(2,1)}) %reduce-scatter.7.cloned.1.call-update) | async-done | bytes 16400 | tf_op jit(solution)/shard_map/reduce_scatter | solution.py:69
  574.6 1.6 fusion.15
  576.3 71.8 %all-reduce.12.cloned.1.call-done = bf16[512,128]{0,1:T(8,128)(2,1)} async-done(((bf16[512,128]{0,1:T(8,128)(2,1)}), bf16[512,128]{0,1:T(8,128)(2,1)}) %all-reduce.12.cloned.1.call-update) | async-done | bytes 131088 | tf_op jit(solution)/shard_map/psum | solution.py:78
  648.1 0.8 constant_dynamic-slice_fusion
  649.0 0.1 copy.42
  649.1 1.8 fusion.11
  651.0 62.1 %reduce-scatter.9.cloned.1.call-done = bf16[64,128]{1,0:T(8,128)(2,1)} async-done(((bf16[512,128]{1,0:T(8,128)(2,1)}), bf16[64,128]{1,0:T(8,128)(2,1)}) %reduce-scatter.9.cloned.1.call-update) | async-done | bytes 16400 | tf_op jit(solution)/shard_map/reduce_scatter | solution.py:69
  713.0 1.6 fusion.16
  714.7 71.8 %all-reduce.14.cloned.1.call-done = bf16[512,128]{0,1:T(8,128)(2,1)} async-done(((bf16[512,128]{0,1:T(8,128)(2,1)}), bf16[512,128]{0,1:T(8,128)(2,1)}) %all-reduce.14.cloned.1.call-update) | async-done | bytes 131088 | tf_op jit(solution)/shard_map/psum | solution.py:78
  786.5 1.0 pad_maximum_fusion
  787.6 1.4 gather_fusion.1
  789.0 1.5 fusion.7
  790.5 1.3 copy.43
  791.8 2.4 fusion.90
  794.2 0.9 copy.53
  795.2 0.1 copy.47
  795.3 0.9 dynamic-slice_convert_fusion
  796.3 0.7 pad_maximum_fusion.1
  796.9 19.1 %reduce-scatter.11.cloned.1.call-done = bf16[1,512,128]{2,1,0:T(8,128)(2,1)} async-done(((bf16[4,512,128]{2,1,0:T(8,128)(2,1)}), bf16[1,512,128]{2,1,0:T(8,128)(2,1)}) %reduce-scatter.11.cloned.1.call-update) | async-done | bytes 131088 | tf_op jit(solution)/shard_map/reduce_scatter | solution.py:89
  816.0 1.2 convolution_bitcast_fusion
  817.2 0.8 copy.49
  (69 shorter events, 1.0 us)
Async XLA Ops:
  7.2 12.3 %copy-start = (bf16[1,4,512,512]{3,2,1,0:T(8,128)(2,1)S(1)}, bf16[1,4,512,512]{3,2,1,0:T(8,128)(2,1)}, u32[]{:S(2)}) copy-start(bf16[1,4,512,512]{3,2,1,0:T(8,128)(2,1)} %param.10) | copy-start | bytes 6291460
  7.2 92.4 %all-reduce.18.cloned.1.call-start = ((), (), s32[]{:S(2)}) async-start(), calls=%async_computation.17 | async-start | bytes 1048576
  19.5 3.3 copy-start.15
  21.4 4.6 copy-start.17
  21.4 125.4 %copy-start.2 = (bf16[4,64,512]{2,1,0:T(8,128)(2,1)S(1)}, bf16[4,64,512]{2,1,0:T(8,128)(2,1)}, u32[]{:S(2)}) copy-start(bf16[4,64,512]{2,1,0:T(8,128)(2,1)} %param.14) | copy-start | bytes 786436
  22.7 111.3 %copy-start.14 = (bf16[4,64,128]{2,1,0:T(8,128)(2,1)S(1)}, bf16[4,64,128]{2,1,0:T(8,128)(2,1)}, u32[]{:S(2)}) copy-start(bf16[4,64,128]{2,1,0:T(8,128)(2,1)} %param.13) | copy-start | bytes 196612
  22.7 154.8 %copy-start.3 = (bf16[6,64,512]{2,1,0:T(8,128)(2,1)S(1)}, bf16[6,64,512]{2,1,0:T(8,128)(2,1)}, u32[]{:S(2)}) copy-start(bf16[6,64,512]{2,1,0:T(8,128)(2,1)} %param.15) | copy-start | bytes 1179652
  25.9 107.3 %all-reduce.16.cloned.1.call-start = ((), (), s32[]{:S(2)}) async-start(), calls=%async_computation.16 | async-start | bytes 131072 | tf_op jit(solution)/shard_map/psum | solution.py:28
  218.3 155.4 %copy-start.12 = (bf16[512,128]{1,0:T(8,128)(2,1)}, bf16[512,128]{1,0:T(8,128)(2,1)S(1)}, u32[]{:S(2)}) copy-start(bf16[512,128]{1,0:T(8,128)(2,1)S(1)} %all_gather.17) | copy-start | bytes 393220
  259.8 0.7 copy-start.13
  261.4 387.7 %slice-start = ((bf16[6,64,512]{2,1,0:T(8,128)(2,1)}), bf16[2,64,512]{2,1,0:T(8,128)(2,1)S(1)}, s32[]{:S(2)}) async-start(bf16[6,64,512]{2,1,0:T(8,128)(2,1)} %param.15), calls=%async_computation.18 | async-start | bytes 262144 | tf_op jit(solution)/shard_map/slice | solution.py:62
  262.0 388.9 %copy-start.16 = (s32[1,4]{1,0:T(1,128)S(1)}, s32[1,4]{1,0:T(1,128)}, u32[]{:S(2)}) copy-start(s32[1,4]{1,0:T(1,128)} %param.12) | copy-start | bytes 52
  262.0 10.9 %all-to-all-start.3 = ((bf16[8,64,128]{2,1,0:T(8,128)(2,1)}), bf16[8,64,128]{2,1,0:T(8,128)(2,1)S(1)}, u32[]{:S(2)}, u32[]{:S(2)}) async-start(bf16[8,64,128]{2,1,0:T(8,128)(2,1)} %stack.130), calls=%async_computation.3 | async-start | bytes 262144 | tf_op jit(solution)/shard_map/all_to_all | solution.py:47
  265.6 106.3 %all-reduce.8.cloned.1.call-start = ((), (), s32[]{:S(2)}) async-start(), calls=%async_computation.8 | async-start | bytes 262144 | tf_op jit(solution)/shard_map/psum | solution.py:78
  304.6 132.0 %reduce-scatter.5.cloned.1.call-start = ((), (), s32[]{:S(2)}) async-start(), calls=%async_computation.9 | async-start | bytes 147456 | tf_op jit(solution)/shard_map/reduce_scatter | solution.py:69
  371.8 414.7 %copy-start.10 = (bf16[512,128]{0,1:T(8,128)(2,1)S(1)}, bf16[512,128]{0,1:T(8,128)(2,1)}, u32[]{:S(2)}) copy-start(bf16[512,128]{0,1:T(8,128)(2,1)} %all-reduce.8.cloned.1.call-done) | copy-start | bytes 393220
  372.7 414.8 %copy-start.4 = (bf16[64,128]{0,1:T(8,128)(2,1)}, bf16[64,128]{0,1:T(8,128)(2,1)S(1)}, u32[]{:S(2)}) copy-start(bf16[64,128]{0,1:T(8,128)(2,1)S(1)} %constant_dynamic-slice_fusion.2) | copy-start | bytes 49156
  373.7 136.2 %all-reduce.10.cloned.1.call-start = ((), (), s32[]{:S(2)}) async-start(), calls=%async_computation.10 | async-start | bytes 262144 | tf_op jit(solution)/shard_map/psum | solution.py:78
  438.2 136.4 %reduce-scatter.7.cloned.1.call-start = ((), (), s32[]{:S(2)}) async-start(), calls=%async_computation.11 | async-start | bytes 147456 | tf_op jit(solution)/shard_map/reduce_scatter | solution.py:69
  509.9 276.6 %copy-start.11 = (bf16[512,128]{0,1:T(8,128)(2,1)S(1)}, bf16[512,128]{0,1:T(8,128)(2,1)}, u32[]{:S(2)}) copy-start(bf16[512,128]{0,1:T(8,128)(2,1)} %all-reduce.10.cloned.1.call-done) | copy-start | bytes 393220
  510.8 276.8 %copy-start.6 = (bf16[64,128]{0,1:T(8,128)(2,1)}, bf16[64,128]{0,1:T(8,128)(2,1)S(1)}, u32[]{:S(2)}) copy-start(bf16[64,128]{0,1:T(8,128)(2,1)S(1)} %constant_dynamic-slice_fusion.1) | copy-start | bytes 49156
  512.7 135.4 %all-reduce.12.cloned.1.call-start = ((), (), s32[]{:S(2)}) async-start(), calls=%async_computation.12 | async-start | bytes 262144 | tf_op jit(solution)/shard_map/psum | solution.py:78
  576.3 136.8 %reduce-scatter.9.cloned.1.call-start = ((), (), s32[]{:S(2)}) async-start(), calls=%async_computation.13 | async-start | bytes 147456 | tf_op jit(solution)/shard_map/reduce_scatter | solution.py:69
  649.0 138.6 %copy-start.8 = (bf16[64,128]{0,1:T(8,128)(2,1)}, bf16[64,128]{0,1:T(8,128)(2,1)S(1)}, u32[]{:S(2)}) copy-start(bf16[64,128]{0,1:T(8,128)(2,1)S(1)} %constant_dynamic-slice_fusion) | copy-start | bytes 49156
  650.9 135.7 %all-reduce.14.cloned.1.call-start = ((), (), s32[]{:S(2)}) async-start(), calls=%async_computation.14 | async-start | bytes 262144 | tf_op jit(solution)/shard_map/psum | solution.py:78
  714.6 101.4 %reduce-scatter.11.cloned.1.call-start = ((), (), s32[]{:S(2)}) async-start(), calls=%async_computation.15 | async-start | bytes 655360 | tf_op jit(solution)/shard_map/reduce_scatter | solution.py:89
  791.8 3.3 copy-start.5
  791.8 3.4 copy-start.7
  791.8 3.5 copy-start.9
  791.8 24.2 %copy-start.1 = (bf16[1,512,512]{2,1,0:T(8,128)(2,1)S(1)}, bf16[1,512,512]{2,1,0:T(8,128)(2,1)}, u32[]{:S(2)}) copy-start(bf16[1,512,512]{2,1,0:T(8,128)(2,1)} %param.9) | copy-start | bytes 1572868
Sparse Core Ops, SparseCore 0:
  26.1 73.4 all-reduce.17
  102.4 30.7 all-reduce.15
  304.7 67.1 all-reduce.7
  375.6 60.9 reduce-scatter.4
  440.3 69.5 all-reduce.9
  513.6 60.9 reduce-scatter.6
  578.6 69.5 all-reduce.11
  652.0 60.9 reduce-scatter.8
  717.0 69.5 all-reduce.13
  795.2 20.7 reduce-scatter.10
